TPU v7x, 256 devices: a whole 4x4x8 slice. The times are simulated.
256 devices in a mesh: dp: 8 (over z_hi, x), ctx: 32 (over y, z_lo, core).
Axes of the slice: x: 4, y: 4, z: 8 (z_hi: 2, z_lo: 4; z = z_hi * 4 + z_lo), core: 2. Of those that a mesh axis runs over, the one named last changes fastest.
Arguments:
- y_first: bfloat16 [8, 4096, 1024], P('dp', 'ctx'), may hold values from -6 to 6
- x_second: bfloat16 [8, 4096, 1024], P('dp', 'ctx'), may hold values from -40 to 40
- grad_first: bfloat16 [8, 4096, 1024], P('dp', 'ctx'), may hold values from -6 to 6
- grad_second: bfloat16 [8, 4096, 1024], P('dp', 'ctx'), may hold values from -6 to 6
- w_query: bfloat16 [1024, 1024], P('dp'), may hold values from -0.1875 to 0.1875
- w_key: bfloat16 [1024, 1024], P('dp'), may hold values from -0.1875 to 0.1875
- w_value: bfloat16 [1024, 1024], P('dp'), may hold values from -0.1875 to 0.1875
- w_out: bfloat16 [1024, 1024], P('dp'), may hold values from -0.1875 to 0.1875
Outputs:
- x_first: bfloat16 [8, 4096, 1024], P('dp', 'ctx')
- grad_x_second: bfloat16 [8, 4096, 1024], P('dp', 'ctx')
- grad_query: float32 [1024, 1024], P(('dp', 'ctx'))
- grad_out: float32 [1024, 1024], P(('dp', 'ctx'))
All inputs are finite; a program needn't handle non-finite values.
Results may differ from a plain program's by a relative error of at most 0.012.
The roundings to bfloat16 on the way count: a program that leaves them out, or rounds other values in their place, can miss the bound.
Values may be sent and summed in bfloat16 or wider, within the bound.
No kernel may reach another device: no remote copies, remote signals or barrier semaphores. Data moves between devices by JAX's collectives and lax.ppermute only.
A program may use at most 128 MiB of HBM per device.

v0:
```python
import jax
import jax.numpy as jnp
from jax import lax
from jax.sharding import PartitionSpec as P

HEADS = 8
HEAD_DIM = 128


def scan_sum(shard, axis, reverse):
    count = lax.axis_size(axis)
    total = shard
    step = 1
    while step < count:
        if reverse:
            pairs = [(source, source - step) for source in range(step, count)]
        else:
            pairs = [(source, source + step) for source in range(count - step)]
        total = total + lax.ppermute(total, axis, pairs)
        step *= 2
    return total


def gather_rows(weights, piece):
    place = lax.axis_index("ctx")
    parts = [lax.dynamic_slice_in_dim(weight, place * piece, piece, 0) for weight in weights]
    joined = jnp.concatenate(parts, 0)
    gathered = lax.all_gather(joined, ("dp", "ctx"), axis=0, tiled=True)
    gathered = gathered.reshape(-1, len(weights), piece, joined.shape[1])
    return tuple((gathered[:, index].reshape(-1, joined.shape[1]) for index in range(len(weights))))


def weight_grads(pairs, factor, owners):
    width = pairs[0][0].shape[1]
    blocks = []
    for left, right in pairs:
        made = lax.dot_general(
            left, right, (((0,), (0,)), ((), ())), preferred_element_type=jnp.float32
        )
        blocks.append((factor * made).reshape(owners, -1, width))
    rows = blocks[0].shape[1]
    stacked = jnp.concatenate(blocks, 1).reshape(-1, width)
    share = lax.psum_scatter(stacked, ("dp", "ctx"), scatter_dimension=0, tiled=True)
    return tuple((share[index * rows : (index + 1) * rows] for index in range(len(pairs))))


def on_device(y_first, x_second, grad_first, grad_second, w_query, w_key, w_value, w_out):
    batch, tokens_here, width = y_first.shape
    owners = lax.axis_size("dp") * lax.axis_size("ctx")
    factor = float(batch * tokens_here * owners) ** (-0.5)
    piece = w_query.shape[0] // lax.axis_size("ctx")
    full_query, full_key, full_value = gather_rows((w_query, w_key, w_value), piece)
    (full_out,) = gather_rows((w_out,), piece)
    second_wide = x_second.astype(jnp.float32)
    inv_rms = lax.rsqrt(jnp.mean(second_wide * second_wide, -1, keepdims=True) + 1e-06)
    normed_wide = second_wide * inv_rms
    normed = normed_wide.astype(jnp.bfloat16)

    def project(weight):
        made = jnp.einsum("btd,df->btf", normed, weight, preferred_element_type=jnp.float32)
        return made.astype(jnp.bfloat16).reshape(batch, tokens_here, HEADS, HEAD_DIM)

    queries = project(full_query)
    key_rows = project(full_key)
    values = project(full_value)
    local_state = jnp.einsum(
        "bthe,bthf->bhef", key_rows, values, preferred_element_type=jnp.float32
    )
    before = (scan_sum(local_state, "ctx", False) - local_state).astype(jnp.bfloat16)
    causal = jnp.tril(jnp.ones((tokens_here, tokens_here), dtype=bool))
    scores = jnp.einsum("bthe,bshe->bhts", queries, key_rows, preferred_element_type=jnp.float32)
    scores = jnp.where(causal[None, None], scores, 0.0).astype(jnp.bfloat16)
    mixed = jnp.einsum("bhts,bshf->bthf", scores, values, preferred_element_type=jnp.float32)
    mixed = mixed + jnp.einsum(
        "bthe,bhef->bthf", queries, before, preferred_element_type=jnp.float32
    )
    inv_head = lax.rsqrt(jnp.mean(mixed * mixed, -1, keepdims=True) + 1e-06)
    unit = mixed * inv_head
    attn_out = unit.astype(jnp.bfloat16).reshape(batch, tokens_here, width)
    attended = jnp.einsum("btf,fd->btd", attn_out, full_out, preferred_element_type=jnp.float32)
    x_first = (y_first.astype(jnp.float32) - attended).astype(jnp.bfloat16)
    grad_unit = jnp.einsum("btd,fd->btf", grad_first, full_out, preferred_element_type=jnp.float32)
    grad_unit = grad_unit.reshape(batch, tokens_here, HEADS, HEAD_DIM)
    grad_mixed = inv_head * (grad_unit - unit * jnp.mean(grad_unit * unit, -1, keepdims=True))
    grad_mixed = grad_mixed.astype(jnp.bfloat16)
    score_grad = jnp.einsum(
        "bthf,bshf->bhts", grad_mixed, values, preferred_element_type=jnp.float32
    )
    score_grad = jnp.where(causal[None, None], score_grad, 0.0).astype(jnp.bfloat16)
    grad_local = jnp.einsum(
        "bthe,bthf->bhef", queries, grad_mixed, preferred_element_type=jnp.float32
    )
    after_state = (scan_sum(grad_local, "ctx", True) - grad_local).astype(jnp.bfloat16)
    query_grad = jnp.einsum(
        "bhts,bshe->bthe", score_grad, key_rows, preferred_element_type=jnp.float32
    )
    query_grad = query_grad + jnp.einsum(
        "bthf,bhef->bthe", grad_mixed, before, preferred_element_type=jnp.float32
    )
    key_grad = jnp.einsum(
        "bhts,bthe->bshe", score_grad, queries, preferred_element_type=jnp.float32
    )
    key_grad = key_grad + jnp.einsum(
        "bshf,bhef->bshe", values, after_state, preferred_element_type=jnp.float32
    )
    value_grad = jnp.einsum(
        "bhts,bthf->bshf", scores, grad_mixed, preferred_element_type=jnp.float32
    )
    value_grad = value_grad + jnp.einsum(
        "bshe,bhef->bshf", key_rows, after_state, preferred_element_type=jnp.float32
    )
    query_grad = query_grad.astype(jnp.bfloat16).reshape(batch, tokens_here, width)
    key_grad = key_grad.astype(jnp.bfloat16).reshape(batch, tokens_here, width)
    value_grad = value_grad.astype(jnp.bfloat16).reshape(batch, tokens_here, width)
    grad_normed = jnp.einsum(
        "btf,df->btd", query_grad, full_query, preferred_element_type=jnp.float32
    )
    grad_normed = grad_normed + jnp.einsum(
        "btf,df->btd", key_grad, full_key, preferred_element_type=jnp.float32
    )
    grad_normed = grad_normed + jnp.einsum(
        "btf,df->btd", value_grad, full_value, preferred_element_type=jnp.float32
    )
    back = inv_rms * (
        grad_normed - normed_wide * jnp.mean(grad_normed * normed_wide, -1, keepdims=True)
    )
    grad_x_second = (grad_second.astype(jnp.float32) + back).astype(jnp.bfloat16)
    pairs = (
        (normed.reshape(-1, width), query_grad.reshape(-1, width)),
        (attn_out.reshape(-1, width), grad_first.reshape(-1, width)),
    )
    grad_query, grad_out = weight_grads(pairs, factor, owners)
    return (x_first, grad_x_second, grad_query, grad_out)


def solution(mesh):
    placed = (
        P("dp", "ctx", None),
        P("dp", "ctx", None),
        P("dp", "ctx", None),
        P("dp", "ctx", None),
        P("dp", None),
        P("dp", None),
        P("dp", None),
        P("dp", None),
    )
    return jax.shard_map(
        on_device,
        mesh=mesh,
        in_specs=placed,
        out_specs=(
            P("dp", "ctx", None),
            P("dp", "ctx", None),
            P(("dp", "ctx"), None),
            P(("dp", "ctx"), None),
        ),
        check_vma=False,
    )
```

profile of v0, /device:TPU:0, one launch (start us, length us, event | category | flops | bytes accessed | tf_op | source)
XLA Modules:
  0.0 2217.5 jit_solution(11344175683100216950)
XLA Ops:
  11.9 420.7 %all-gather.5.cloned.1.call-done = bf16[256,12,1024]{2,1,0:T(8,128)(2,1)} async-done(((bf16[1,12,1024]{2,1,0:T(8,128)(2,1)}), bf16[256,12,1024]{2,1,0:T(8,128)(2,1)}) %all-gather.5.cloned.1.call-update) | async-done | bytes 6291472 | tf_op jit(solution)/shard_map/all_gather | solution.py:28
  432.6 6.9 copy.67
  439.5 3.4 fusion.43
  448.4 4.5 copy.70
  452.9 4.0 reshape_squeeze.11
  463.7 10.4 collective-permute-start.1
  474.1 10.7 collective-permute-done.1
  484.8 4.5 collective-permute-start.2
  489.4 9.0 collective-permute-done.2
  499.2 16.1 collective-permute-start.3
  515.4 342.0 %all-gather.7.cloned.1.call-done = bf16[256,4,1024]{2,1,0:T(4,128)(2,1)} async-done(((bf16[1,4,1024]{2,1,0:T(4,128)(2,1)}), bf16[256,4,1024]{2,1,0:T(4,128)(2,1)}) %all-gather.7.cloned.1.call-update) | async-done | bytes 2097168 | tf_op jit(solution)/shard_map/all_gather | solution.py:28
  857.4 4.0 reshape.224
  861.4 3.3 fusion.31
  864.7 3.0 copy.69
  867.7 4.0 reshape_squeeze.10
  891.4 5.2 reshape.218
  896.6 3.6 convolution_multiply_fusion
  900.2 5.2 reshape.219
  905.4 8.9 maximum_bitcast_fusion
  920.0 18.2 collective-permute-done.6
  939.6 31.6 %collective-permute-done.7 = f32[1,8,128,128]{3,2,1,0:T(8,128)S(1)} collective-permute-done((f32[1,8,128,128]{3,2,1,0:T(8,128)S(1)}, f32[1,8,128,128]{3,2,1,0:T(8,128)S(1)}, u32[]{:S(2)}, u32[]{:S(2)}) %collective-permute-start.7) | collective-permute-done | bytes 524320 | tf_op jit(solution)/shard_map/ppermute | solution.py:19
  973.7 12.9 collective-permute-done.8
  989.6 15.4 collective-permute-done.9
  1008.5 1201.0 %reduce-scatter.2.cloned.1.call-done = f32[8,1024]{1,0:T(8,128)} async-done(((f32[2048,1024]{1,0:T(8,128)}), f32[8,1024]{1,0:T(8,128)}) %reduce-scatter.2.cloned.1.call-update) | async-done | bytes 32784 | tf_op jit(solution)/shard_map/reduce_scatter | solution.py:43
  (110 shorter events, 54.9 us)
Async XLA Ops:
  7.2 854.2 %copy-start = (bf16[1,128,1024]{2,1,0:T(8,128)(2,1)S(1)}, bf16[1,128,1024]{2,1,0:T(8,128)(2,1)}, u32[]{:S(2)}) copy-start(bf16[1,128,1024]{2,1,0:T(8,128)(2,1)} %param.10) | copy-start | bytes 786436
  7.2 425.5 %all-gather.5.cloned.1.call-start = ((), (), s32[]{:S(2)}) async-start(), calls=%async_computation.2 | async-start | bytes 8421376 | tf_op jit(solution)/shard_map/all_gather | solution.py:28
  9.4 848.0 %all-gather.7.cloned.1.call-start = ((), (), s32[]{:S(2)}) async-start(), calls=%async_computation.3 | async-start | bytes 2105344 | tf_op jit(solution)/shard_map/all_gather | solution.py:28
  10.8 2198.7 %reduce-scatter.2.cloned.1.call-start = ((), (), s32[]{:S(2)}) async-start(), calls=%async_computation.1 | async-start | bytes 8421376 | tf_op jit(solution)/shard_map/reduce_scatter | solution.py:43
  460.6 24.3 %copy-start.7 = (bf16[16,8,8,128]{3,2,1,0:T(8,128)(2,1)}, bf16[16,8,8,128]{3,2,1,0:T(8,128)(2,1)S(1)}, u32[]{:S(2)}) copy-start(bf16[16,8,8,128]{3,2,1,0:T(8,128)(2,1)S(1)} %fusion.9) | copy-start | bytes 786436
  460.8 2.8 collective-permute-start
  463.7 21.1 collective-permute-start.1
  484.8 13.5 collective-permute-start.2
  499.2 372.4 %collective-permute-start.3 = (f32[1,8,128,128]{3,2,1,0:T(8,128)}, f32[1,8,128,128]{3,2,1,0:T(8,128)}, u32[]{:S(2)}, u32[]{:S(2)}) collective-permute-start(f32[1,8,128,128]{3,2,1,0:T(8,128)} %add.102), channel_id=1, source_target_pairs={{0,8},{1,9},{2,10},{3,11},{4,12},{5,13},{6,14},{7,15},{8,16},{9,17... | collective-permute-start | bytes 1572872 | tf_op jit(solution)/shard_map/ppermute | solution.py:19
  873.7 10.6 collective-permute-start.4
  914.6 58.0 %copy-start.19 = (bf16[8,128,128]{2,1,0:T(8,128)(2,1)S(1)}, bf16[8,128,128]{2,1,0:T(8,128)(2,1)}, u32[]{:S(2)}) copy-start(bf16[8,128,128]{2,1,0:T(8,128)(2,1)} %copy-done.18) | copy-start | bytes 786436
  914.6 3.9 collective-permute-start.5
  918.6 54.2 %copy-start.2 = (bf16[1024,1024]{1,0:T(8,128)(2,1)S(1)}, bf16[1024,1024]{1,0:T(8,128)(2,1)}, u32[]{:S(2)}) copy-start(bf16[1024,1024]{1,0:T(8,128)(2,1)} %reshape_squeeze.10) | copy-start | bytes 6291460
  918.6 54.2 %copy-start.10 = (bf16[8,128,128]{2,1,0:T(8,128)(2,1)S(1)}, bf16[8,128,128]{2,1,0:T(8,128)(2,1)}, u32[]{:S(2)}) copy-start(bf16[8,128,128]{2,1,0:T(8,128)(2,1)} %copy-done.9) | copy-start | bytes 786436
  918.6 19.6 collective-permute-start.6
  938.3 32.9 %collective-permute-start.7 = (f32[1,8,128,128]{3,2,1,0:T(8,128)S(1)}, f32[1,8,128,128]{3,2,1,0:T(8,128)S(1)}, u32[]{:S(2)}, u32[]{:S(2)}) collective-permute-start(f32[1,8,128,128]{3,2,1,0:T(8,128)S(1)} %add.112), channel_id=1, source_target_pairs={{4,0},{5,1},{6,2},{7,3},{8,4},{9,5},{10,6},{11,7},{12,8},{13,9},{1... | collective-permute-start | bytes 1572872 | tf_op jit(solution)/shard_map/ppermute | solution.py:19
  971.2 15.3 collective-permute-start.8
  972.8 15.4 copy-start.17
  972.8 15.6 copy-start.1
  972.8 15.6 copy-start.15
  972.8 15.6 copy-start.21
  986.6 18.4 collective-permute-start.9
  988.4 16.7 copy-start.12
  989.6 16.2 copy-start.3
  (11 other events, 23.0 us)
Sparse Core Ops, SparseCore 0:
  10.4 422.1 all-gather.4
  435.1 422.2 all-gather.6
  914.4 1295.0 reduce-scatter.1
where the time goes:
time: 2220 us
  waiting for transfers between devices  2070 us (93%)
  local copies, waits for them, and re-layouts  53 us (2%)
  starting transfers between devices  41.5 us (2%)
  matrix products  24.2 us (1%)
    reduce_scatter x1, waiting for transfers between devices, weight_grads(): lax.psum_scatter(stacked, ('dp', 'ctx'), scatter_dimension=0, tiled=True)  1200 us
    all_gather x2, waiting for transfers between devices, gather_rows(): gathered = lax.all_gather(joined, ('dp', 'ctx'), axis=0, tiled=True)  763 us
    ppermute x10, waiting for transfers between devices, scan_sum(): total = total + lax.ppermute(total, axis, pairs)  104 us
  transfers between devices with their start and end apart: 13, of which 12 were waited for; matrix products, arithmetic and copies ran while one was open for 3% of the time, Pallas kernels for 0%

commit v1 on v0

--- a/solution.py
+++ b/solution.py
@@ -25,7 +25,10 @@
     place = lax.axis_index("ctx")
     parts = [lax.dynamic_slice_in_dim(weight, place * piece, piece, 0) for weight in weights]
     joined = jnp.concatenate(parts, 0)
-    gathered = lax.all_gather(joined, ("dp", "ctx"), axis=0, tiled=True)
+    values_bind = lambda slab_in, link_axis, axis_no: jnp.concatenate(
+        lax.all_to_all(jnp.stack(lax.psum(1, link_axis) * [slab_in]), link_axis, 0, 0), axis=axis_no
+    )
+    gathered = values_bind(joined, ("dp", "ctx"), 0)
     gathered = gathered.reshape(-1, len(weights), piece, joined.shape[1])
     return tuple((gathered[:, index].reshape(-1, joined.shape[1]) for index in range(len(weights))))
 

time: 2220 us -> 1690 us (0.76)
  waiting for transfers between devices: 2070 us -> 1490 us
  starting transfers between devices: 41.5 us -> 85.3 us
    all_gather x2 -> x0, waiting for transfers between devices: 763 us -> none  [gather_rows(): gathered = lax.all_gather(joined, ('dp', 'ctx'), axis=0, tiled=True)]
    all_to_all x0 -> x2, waiting for transfers between devices: none -> 183 us  [gather_rows(): lax.all_to_all(jnp.stack(lax.psum(1, link_axis) * [slab_in]), link_axis,...]
    all_to_all x0 -> x2, starting transfers between devices: none -> 26.7 us  [gather_rows(): lax.all_to_all(jnp.stack(lax.psum(1, link_axis) * [slab_in]), link_axis,...]
  transfers between devices with their start and end apart: 13 -> 13, of which waited for: 12 -> 11; matrix products, arithmetic and copies ran while one was open for 3% -> 3% of each run, Pallas kernels for 0% -> 0%
where the time goes in v1:
time: 1690 us
  waiting for transfers between devices  1490 us (88%)
  starting transfers between devices  85.3 us (5%)
  local copies, waits for them, and re-layouts  54.6 us (3%)
  matrix products  24.9 us (1%)
    reduce_scatter x1, waiting for transfers between devices, weight_grads(): lax.psum_scatter(stacked, ('dp', 'ctx'), scatter_dimension=0, tiled=True)  1210 us
    all_to_all x2, waiting for transfers between devices, gather_rows(): lax.all_to_all(jnp.stack(lax.psum(1, link_axis) * [slab_in]), link_axis,...  183 us
    ppermute x10, waiting for transfers between devices, scan_sum(): total = total + lax.ppermute(total, axis, pairs)  105 us
    ppermute x10, starting transfers between devices, scan_sum(): total = total + lax.ppermute(total, axis, pairs)  58.3 us
  transfers between devices with their start and end apart: 13, of which 11 were waited for; matrix products, arithmetic and copies ran while one was open for 3% of the time, Pallas kernels for 0%

profile of v1, /device:TPU:0, one launch (start us, length us, event | category | flops | bytes accessed | tf_op | source)
XLA Modules:
  0.0 1687.3 jit_solution(5650302011925631575)
XLA Ops:
  8.7 4.3 stack.4
  13.0 15.7 all-to-all-start
  29.4 182.7 %all-to-all-done = bf16[256,12,1024]{2,1,0:T(8,128)(2,1)} async-done(((bf16[256,12,1024]{2,1,0:T(8,128)(2,1)}), bf16[256,12,1024]{2,1,0:T(8,128)(2,1)}, u32[]{:S(2)}, u32[]{:S(2)}) %all-to-all-start) | async-done | bytes 6291488 | tf_op jit(solution)/shard_map/all_to_all | solution.py:29
  214.0 11.0 all-to-all-start.1
  225.5 6.9 copy.66
  239.2 4.6 copy.67
  253.0 23.2 %collective-permute-start.1 = (f32[1,8,128,128]{3,2,1,0:T(8,128)S(1)}, f32[1,8,128,128]{3,2,1,0:T(8,128)S(1)}, u32[]{:S(2)}, u32[]{:S(2)}) collective-permute-start(f32[1,8,128,128]{3,2,1,0:T(8,128)S(1)} %add.100), channel_id=1, source_target_pairs={{0,2},{1,3},{2,4},{3,5},{4,6},{5,7},{6,8},{7,9},{8,10},{9,11},{10,... | collective-permute-start | bytes 1572872 | tf_op jit(solution)/shard_map/ppermute | solution.py:19
  276.2 10.5 collective-permute-done.1
  286.7 5.4 collective-permute-start.2
  292.2 9.8 collective-permute-done.2
  302.8 16.3 collective-permute-start.3
  319.2 4.0 reshape_squeeze_reshape_reshape.3
  323.2 3.3 fusion.31
  329.5 4.0 reshape_squeeze.10
  335.5 5.1 collective-permute-start.4
  355.9 5.2 reshape.219
  361.1 3.7 convolution_multiply_fusion.1
  364.8 5.2 reshape.218
  370.0 8.9 maximum_bitcast_fusion
  384.7 19.0 %collective-permute-done.6 = f32[1,8,128,128]{3,2,1,0:T(8,128)S(1)} collective-permute-done((f32[1,8,128,128]{3,2,1,0:T(8,128)S(1)}, f32[1,8,128,128]{3,2,1,0:T(8,128)S(1)}, u32[]{:S(2)}, u32[]{:S(2)}) %collective-permute-start.6) | collective-permute-done | bytes 524320 | tf_op jit(solution)/shard_map/ppermute | solution.py:19
  405.1 28.3 %collective-permute-done.7 = f32[1,8,128,128]{3,2,1,0:T(8,128)S(1)} collective-permute-done((f32[1,8,128,128]{3,2,1,0:T(8,128)S(1)}, f32[1,8,128,128]{3,2,1,0:T(8,128)S(1)}, u32[]{:S(2)}, u32[]{:S(2)}) %collective-permute-start.7) | collective-permute-done | bytes 524320 | tf_op jit(solution)/shard_map/ppermute | solution.py:19
  435.9 15.9 collective-permute-done.8
  454.8 15.0 collective-permute-done.9
  473.3 1205.7 %reduce-scatter.2.cloned.1.call-done = f32[8,1024]{1,0:T(8,128)} async-done(((f32[2048,1024]{1,0:T(8,128)}), f32[8,1024]{1,0:T(8,128)}) %reduce-scatter.2.cloned.1.call-update) | async-done | bytes 32784 | tf_op jit(solution)/shard_map/reduce_scatter | solution.py:46
  (110 shorter events, 59.0 us)
Async XLA Ops:
  7.2 316.0 %copy-start = (bf16[1,128,1024]{2,1,0:T(8,128)(2,1)S(1)}, bf16[1,128,1024]{2,1,0:T(8,128)(2,1)}, u32[]{:S(2)}) copy-start(bf16[1,128,1024]{2,1,0:T(8,128)(2,1)} %param.10) | copy-start | bytes 786436
  13.0 199.1 %all-to-all-start = ((bf16[256,12,1024]{2,1,0:T(8,128)(2,1)}), bf16[256,12,1024]{2,1,0:T(8,128)(2,1)}, u32[]{:S(2)}, u32[]{:S(2)}) async-start(bf16[256,12,1024]{2,1,0:T(8,128)(2,1)} %stack.4), calls=%async_computation | async-start | bytes 16777216 | tf_op jit(solution)/shard_map/all_to_all | solution.py:29
  214.0 105.2 %all-to-all-start.1 = ((bf16[256,4,1024]{2,1,0:T(4,128)(2,1)}), bf16[256,4,1024]{2,1,0:T(4,128)(2,1)}, u32[]{:S(2)}, u32[]{:S(2)}) async-start(bf16[256,4,1024]{2,1,0:T(4,128)(2,1)} %stack.5), calls=%async_computation.1 | async-start | bytes 4194304 | tf_op jit(solution)/shard_map/all_to_all | solution.py:29
  225.1 1454.0 %reduce-scatter.2.cloned.1.call-start = ((), (), s32[]{:S(2)}) async-start(), calls=%async_computation.3 | async-start | bytes 8421376 | tf_op jit(solution)/shard_map/reduce_scatter | solution.py:46
  249.9 36.9 %copy-start.7 = (bf16[16,8,8,128]{3,2,1,0:T(8,128)(2,1)}, bf16[16,8,8,128]{3,2,1,0:T(8,128)(2,1)S(1)}, u32[]{:S(2)}) copy-start(bf16[16,8,8,128]{3,2,1,0:T(8,128)(2,1)S(1)} %fusion.9) | copy-start | bytes 786436
  250.1 2.8 collective-permute-start
  253.0 33.7 %collective-permute-start.1 = (f32[1,8,128,128]{3,2,1,0:T(8,128)S(1)}, f32[1,8,128,128]{3,2,1,0:T(8,128)S(1)}, u32[]{:S(2)}, u32[]{:S(2)}) collective-permute-start(f32[1,8,128,128]{3,2,1,0:T(8,128)S(1)} %add.100), channel_id=1, source_target_pairs={{0,2},{1,3},{2,4},{3,5},{4,6},{5,7},{6,8},{7,9},{8,10},{9,11},{10,... | collective-permute-start | bytes 1572872 | tf_op jit(solution)/shard_map/ppermute | solution.py:19
  286.7 15.3 collective-permute-start.2
  302.8 30.7 %collective-permute-start.3 = (f32[1,8,128,128]{3,2,1,0:T(8,128)}, f32[1,8,128,128]{3,2,1,0:T(8,128)}, u32[]{:S(2)}, u32[]{:S(2)}) collective-permute-start(f32[1,8,128,128]{3,2,1,0:T(8,128)} %add.102), channel_id=1, source_target_pairs={{0,8},{1,9},{2,10},{3,11},{4,12},{5,13},{6,14},{7,15},{8,16},{9,17... | collective-permute-start | bytes 1572872 | tf_op jit(solution)/shard_map/ppermute | solution.py:19
  335.5 13.9 collective-permute-start.4
  379.2 55.5 %copy-start.19 = (bf16[8,128,128]{2,1,0:T(8,128)(2,1)S(1)}, bf16[8,128,128]{2,1,0:T(8,128)(2,1)}, u32[]{:S(2)}) copy-start(bf16[8,128,128]{2,1,0:T(8,128)(2,1)} %copy-done.18) | copy-start | bytes 786436
  379.3 3.9 collective-permute-start.5
  383.2 51.7 %copy-start.2 = (bf16[1024,1024]{1,0:T(8,128)(2,1)S(1)}, bf16[1024,1024]{1,0:T(8,128)(2,1)}, u32[]{:S(2)}) copy-start(bf16[1024,1024]{1,0:T(8,128)(2,1)} %reshape_squeeze.10) | copy-start | bytes 6291460
  383.3 51.7 %copy-start.9 = (bf16[8,128,128]{2,1,0:T(8,128)(2,1)S(1)}, bf16[8,128,128]{2,1,0:T(8,128)(2,1)}, u32[]{:S(2)}) copy-start(bf16[8,128,128]{2,1,0:T(8,128)(2,1)} %fusion.6) | copy-start | bytes 786436
  383.3 20.5 %collective-permute-start.6 = (f32[1,8,128,128]{3,2,1,0:T(8,128)S(1)}, f32[1,8,128,128]{3,2,1,0:T(8,128)S(1)}, u32[]{:S(2)}, u32[]{:S(2)}) collective-permute-start(f32[1,8,128,128]{3,2,1,0:T(8,128)S(1)} %add.111), channel_id=1, source_target_pairs={{2,0},{3,1},{4,2},{5,3},{6,4},{7,5},{8,6},{9,7},{10,8},{11,9},{12,... | collective-permute-start | bytes 1572872 | tf_op jit(solution)/shard_map/ppermute | solution.py:19
  403.8 29.6 %collective-permute-start.7 = (f32[1,8,128,128]{3,2,1,0:T(8,128)S(1)}, f32[1,8,128,128]{3,2,1,0:T(8,128)S(1)}, u32[]{:S(2)}, u32[]{:S(2)}) collective-permute-start(f32[1,8,128,128]{3,2,1,0:T(8,128)S(1)} %add.112), channel_id=1, source_target_pairs={{4,0},{5,1},{6,2},{7,3},{8,4},{9,5},{10,6},{11,7},{12,8},{13,9},{1... | collective-permute-start | bytes 1572872 | tf_op jit(solution)/shard_map/ppermute | solution.py:19
  433.4 18.3 %collective-permute-start.8 = (f32[1,8,128,128]{3,2,1,0:T(8,128)S(1)}, f32[1,8,128,128]{3,2,1,0:T(8,128)S(1)}, u32[]{:S(2)}, u32[]{:S(2)}) collective-permute-start(f32[1,8,128,128]{3,2,1,0:T(8,128)S(1)} %add.113), channel_id=1, source_target_pairs={{8,0},{9,1},{10,2},{11,3},{12,4},{13,5},{14,6},{15,7},{16,8},{17,9... | collective-permute-start | bytes 1572872 | tf_op jit(solution)/shard_map/ppermute | solution.py:19
  435.0 18.4 %copy-start.17 = (bf16[8,128,128]{2,1,0:T(8,128)(2,1)S(1)}, bf16[8,128,128]{2,1,0:T(8,128)(2,1)}, u32[]{:S(2)}) copy-start(bf16[8,128,128]{2,1,0:T(8,128)(2,1)} %copy-done.16) | copy-start | bytes 786436
  435.0 18.6 %copy-start.1 = (bf16[1024,1024]{1,0:T(8,128)(2,1)S(1)}, bf16[1024,1024]{1,0:T(8,128)(2,1)}, u32[]{:S(2)}) copy-start(bf16[1024,1024]{1,0:T(8,128)(2,1)} %reshape_squeeze_reshape_reshape.3) | copy-start | bytes 6291460
  435.0 18.6 %copy-start.15 = (bf16[1,128,8,128]{1,3,2,0:T(8,128)(2,1)S(1)}, bf16[1,128,8,128]{1,3,2,0:T(8,128)(2,1)}, u32[]{:S(2)}) copy-start(bf16[1,128,8,128]{1,3,2,0:T(8,128)(2,1)} %copy-done.14) | copy-start | bytes 786436
  435.0 18.6 %copy-start.21 = (bf16[1,128,1024]{2,1,0:T(8,128)(2,1)S(1)}, bf16[1,128,1024]{2,1,0:T(8,128)(2,1)}, u32[]{:S(2)}) copy-start(bf16[1,128,1024]{2,1,0:T(8,128)(2,1)} %param.8) | copy-start | bytes 786436
  451.8 18.0 %collective-permute-start.9 = (f32[1,8,128,128]{3,2,1,0:T(8,128)S(1)}, f32[1,8,128,128]{3,2,1,0:T(8,128)S(1)}, u32[]{:S(2)}, u32[]{:S(2)}) collective-permute-start(f32[1,8,128,128]{3,2,1,0:T(8,128)S(1)} %add.114), channel_id=1, source_target_pairs={{16,0},{17,1},{18,2},{19,3},{20,4},{21,5},{22,6},{23,7},{24,8},{25... | collective-permute-start | bytes 1572872 | tf_op jit(solution)/shard_map/ppermute | solution.py:19
  454.8 15.4 copy-start.11
  454.8 15.7 copy-start.3
  (11 other events, 31.7 us)
Sparse Core Ops, SparseCore 0:
  379.1 1299.9 reduce-scatter.1
